TPU v7x, 32 devices: a whole 2x2x4 slice. The times are simulated.
32 devices in a mesh: groups: 2 (over y), gz: 4 (over z), sec: 2 (over x), ch: 2 (over core).
Axes of the slice: x: 2, y: 2, z: 4, core: 2. Of those that a mesh axis runs over, the one named last changes fastest.
Arguments:
- coarse: bfloat16 [64, 32, 4, 256], P('ch', ('groups', 'gz', 'sec')), parts along dimension 1, may hold values from -6 to 6
- saved_pre: bfloat16 [32, 64, 8, 512], P('ch', ('groups', 'gz', 'sec')), parts along dimension 1, may hold values from -6 to 6
- out_grad: bfloat16 [32, 64, 8, 512], P('ch', ('groups', 'gz', 'sec')), parts along dimension 1, may hold values from -6 to 6
- up_weight: bfloat16 [27, 32, 64], replicated, may hold values from -0.21875 to 0.21875
- refine_weight: bfloat16 [27, 32, 32], replicated, may hold values from -0.21875 to 0.21875
Outputs:
- grad_coarse: bfloat16 [64, 32, 4, 256], P('ch', ('groups', 'gz', 'sec')), parts along dimension 1
- grad_up: float32 [54, 32, 64], P('groups', 'ch'), parts along dimension 0
- grad_refine: float32 [54, 32, 32], P('groups', None, 'ch'), parts along dimension 0
There are 2 independent parts, one for each index of `groups`. A program takes and returns all parts, laid end to end along the dimension named above; an argument that names none is the same for every part. Nothing has to cross between parts.
All inputs are finite; a program needn't handle non-finite values.
Results may differ from a plain program's by a relative error of at most 0.0049.
Values may be sent and summed in bfloat16 or wider, within the bound.
No kernel may reach another device: no remote copies, remote signals or barrier semaphores. Data moves between devices by JAX's collectives and lax.ppermute only.
A program may use at most 128 MiB of HBM per device.

v0:
```python
import jax
import jax.numpy as jnp
from jax import lax
from jax.sharding import PartitionSpec as P

leak_slope = 0.2
SPATIAL = ("NCDHW", "OIDHW", "NCDHW")


def padded(block, sides, width):
    for axis, dim in sides:
        count = lax.axis_size(axis)
        forward = [(i, i + 1) for i in range(count - 1)]
        forward.append((count - 1, 0))
        backward = [(target, source) for source, target in forward]
        low = lax.ppermute(
            lax.slice_in_dim(block, block.shape[dim] - width, None, axis=dim), axis, forward
        )
        high = lax.ppermute(lax.slice_in_dim(block, 0, width, axis=dim), axis, backward)
        block = jnp.concatenate([low, block, high], axis=dim)
    return block


def passed_along(block, axis, distance):
    devices = range(lax.axis_size(axis))
    route = [((i - distance) % len(devices), i) for i in devices]
    return lax.ppermute(block, axis, route)


def wrap_y(block, low, high):
    size = block.shape[3]
    parts = [block[:, :, :, size - low :], block, block[:, :, :, :high]]
    return jnp.concatenate([p for p in parts if p.shape[3]], axis=3)


def conv(lhs, rhs, strides, dilation):
    return lax.conv_general_dilated(
        lhs,
        rhs,
        window_strides=strides,
        padding="VALID",
        rhs_dilation=dilation,
        dimension_numbers=SPATIAL,
        preferred_element_type=jnp.float32,
    )


def filter_grad(lhs, cotangent, strides, dilation):
    return lax.conv_general_dilated(
        lhs,
        cotangent,
        window_strides=strides,
        padding="VALID",
        rhs_dilation=dilation,
        dimension_numbers=("CNDHW", "IODHW", "CNDHW"),
        preferred_element_type=jnp.float32,
    )


def local(coarse, saved_pre, out_grad, up_weight, refine_weight):
    part_ch = saved_pre.shape[0]
    planes_z = saved_pre.shape[1]
    planes_x = saved_pre.shape[2]
    cells_y = saved_pre.shape[3]
    channel_start = lax.axis_index("ch") * part_ch
    pre_act = saved_pre.astype(jnp.float32)
    slopes = jnp.where(pre_act > 0, 1.0, leak_slope).astype(jnp.float32)
    hidden = (pre_act * slopes).astype(jnp.bfloat16)
    rimmed_local = padded(out_grad, ((("gz", "sec"), 1),), 2)
    every_channel = lax.all_gather(rimmed_local, "ch", axis=0, tiled=True)
    rimmed = jnp.pad(every_channel, ((0, 0), (0, 0), (2, 2), (0, 0)))
    rimmed = wrap_y(rimmed, 2, 2)[None]
    refine_cols = lax.dynamic_slice_in_dim(refine_weight, channel_start, part_ch, 2)
    refine_k = refine_cols.reshape(3, 3, 3, refine_cols.shape[1], part_ch)[::-1, ::-1, ::-1]
    refine_k = jnp.transpose(refine_k, (4, 3, 0, 1, 2))
    grad_hidden = conv(rimmed, refine_k, (1, 1, 1), (2, 2, 2))[0]
    refine_grad_k = filter_grad(rimmed, hidden[None], (2, 2, 2), (1, 1, 1))
    refine_terms = jnp.transpose(refine_grad_k[:, :, ::-1, ::-1, ::-1], (2, 3, 4, 1, 0))
    refine_terms = refine_terms.reshape(27, refine_cols.shape[1], part_ch)
    grad_pre = (grad_hidden * slopes).astype(jnp.bfloat16)
    below_z = passed_along(grad_pre[:, planes_z - 1 :, :, :], ("gz", "sec"), 1)
    raised_z = jnp.concatenate([below_z, grad_pre], axis=1)
    extended = jnp.pad(raised_z, ((0, 0), (0, 0), (1, 0), (0, 0)))
    extended = wrap_y(extended, 1, 0)[None]
    all_coarse = lax.all_gather(coarse, "ch", axis=0, tiled=True)
    up_rows = lax.dynamic_slice_in_dim(up_weight, channel_start, part_ch, 1)
    up_k = jnp.transpose(up_rows.reshape(3, 3, 3, part_ch, up_rows.shape[2]), (4, 3, 0, 1, 2))
    running = conv(extended, up_k, (2, 2, 2), (1, 1, 1))
    up_grad_k = filter_grad(extended, all_coarse[None], (1, 1, 1), (2, 2, 2))
    up_terms = jnp.transpose(up_grad_k, (2, 3, 4, 1, 0)).reshape(27, part_ch, up_rows.shape[2])
    coarse_summed = lax.psum_scatter(running[0], "ch", scatter_dimension=0, tiled=True)
    grad_coarse = coarse_summed.astype(jnp.bfloat16)
    flat = jnp.concatenate([up_terms.reshape(-1), refine_terms.reshape(-1)])
    flat = lax.psum(flat, ("gz", "sec"))
    up_summed = flat[: up_terms.size].reshape(up_terms.shape)
    refine_summed = flat[up_terms.size :].reshape(refine_terms.shape)
    fine_total = planes_z * lax.axis_size("gz") * lax.axis_size("sec") * planes_x * cells_y
    coarse_total = fine_total // 8
    grad_up = up_summed * float(coarse_total) ** (-0.5)
    grad_refine = refine_summed * float(fine_total) ** (-0.5)
    return (grad_coarse, grad_up, grad_refine)


def solution(mesh):
    placed = (
        P("ch", ("groups", "gz", "sec"), None, None),
        P("ch", ("groups", "gz", "sec"), None, None),
        P("ch", ("groups", "gz", "sec"), None, None),
        P(),
        P(),
    )
    return jax.shard_map(
        local,
        mesh=mesh,
        in_specs=placed,
        out_specs=(
            P("ch", ("groups", "gz", "sec"), None, None),
            P("groups", "ch", None),
            P("groups", None, "ch"),
        ),
        check_vma=False,
    )
```

profile of v0, /device:TPU:0, one launch (start us, length us, event | category | flops | bytes accessed | tf_op | source)
XLA Modules:
  0.0 495.4 jit_solution(4544733990261625754)
XLA Ops:
  7.2 1.2 fusion.36
  8.4 6.0 %collective-permute-start.1 = (bf16[16,2,8,512]{3,2,1,0:T(8,128)(2,1)S(1)}, bf16[16,2,8,512]{3,2,1,0:T(8,128)(2,1)S(1)}, u32[]{:S(2)}, u32[]{:S(2)}) collective-permute-start(bf16[16,2,8,512]{3,2,1,0:T(8,128)(2,1)S(1)} %get-tuple-element.21), channel_id=1, source_target_pairs={{2,0},{4,2},{6,4},{8,6},{10,8},{12,10},{14,12},{0,14},{3,1},{5,3},... | collective-permute-start | bytes 786440 | tf_op jit(solution)/shard_map/ppermute | solution.py:19
  14.4 5.6 %collective-permute-done.1 = bf16[16,2,8,512]{3,2,1,0:T(8,128)(2,1)S(1)} collective-permute-done((bf16[16,2,8,512]{3,2,1,0:T(8,128)(2,1)S(1)}, bf16[16,2,8,512]{3,2,1,0:T(8,128)(2,1)S(1)}, u32[]{:S(2)}, u32[]{:S(2)}) %collective-permute-start.1) | collective-permute-done | bytes 262176 | tf_op jit(solution)/shard_map/ppermute | solution.py:19
  20.0 4.9 collective-permute-done
  24.9 2.1 pad_maximum_fusion.1
  27.1 1.2 dynamic-slice
  29.9 2.0 all_gather.7
  31.9 2.0 copy.65
  34.7 3.3 all-gather.2.cloned.1.call-done
  38.0 2.5 copy.53
  41.2 4.0 fusion.23
  45.2 2.3 pad.10
  47.5 10.9 %reshape.30 = bf16[32,8,12,1,8,65]{5,4,1,2,0,3:T(8,128)(2,1)} reshape(bf16[32,8,12,1,520]{4,1,2,0,3:T(8,128)(2,1)} %pad.10) | data formatting | bytes 6389760 | tf_op jit(solution)/shard_map/conv_general_dilated | solution.py:37
  58.4 17.4 %copy.55 = bf16[32,8,12,1,8,65]{0,4,5,2,1,3:T(8,128)(2,1)} copy(bf16[32,8,12,1,8,65]{5,4,1,2,0,3:T(8,128)(2,1)} %reshape.30) | data formatting | bytes 6389760 | tf_op jit(solution)/shard_map/conv_general_dilated | solution.py:37
  75.8 1.4 slice.44
  77.2 26.3 %broadcast_select_fusion = f32[4,8,8,65,16]{4,2,3,1,0:T(8,128)} fusion(pred[8,65]{0,1:T(8,128)(4,1)S(1)} %copy-done.8, bf16[3,3,3,32,16]{4,3,2,1,0:T(8,128)(2,1)S(1)} %bitcast.62, bf16[32,8,12,1,7,4]{0,4,5,2,1,3:T(8,128)(2,1)S(1)} %slice.44, bf16[32,8,12,1,8,65]{0,4,5,2,1,3:T(8,128)(2,1)} %copy.55), kind=kOutput, calls=%fused_computation.14 | convolution fusion | flops 470503424 | bytes 4460040 | tf_op jit(solution)/shard_map/conv_general_dilated | solution.py:37
  103.5 5.6 %copy.57 = f32[4,8,8,65,16]{3,2,4,1,0:T(8,128)S(1)} copy(f32[4,8,8,65,16]{4,2,3,1,0:T(8,128)} %broadcast_select_fusion) | data formatting | bytes 2129920 | tf_op jit(solution)/shard_map/conv_general_dilated | solution.py:37
  109.1 1.8 reshape.34
  110.9 1.7 fusion.29
  114.1 1.7 collective-permute-start.2
  115.8 43.9 %copy.66 = bf16[1,32,8,12,516]{1,0,4,3,2:T(2,128)(2,1)} copy(bf16[1,32,8,12,516]{4,2,3,1,0:T(8,128)(2,1)} %get-tuple-element.12) | data formatting | bytes 6340608 | tf_op jit(solution)/shard_map/broadcast_in_dim | solution.py:72
  159.7 14.3 %copy.67 = bf16[1,16,4,8,512]{1,0,4,3,2:T(2,128)(2,1)} copy(bf16[1,16,4,8,512]{4,1,3,2,0:T(8,128)(2,1)S(1)} %get-tuple-element.18) | data formatting | bytes 1048576 | tf_op jit(solution)/shard_map/broadcast_in_dim | solution.py:77
  174.0 172.7 %fusion.38 = f32[16,32,3,3,3]{1,0,4,3,2:T(8,128)S(1)} fusion(bf16[1,32,8,12,516]{1,0,4,3,2:T(2,128)(2,1)} %copy.66, bf16[1,16,4,8,512]{1,0,4,3,2:T(2,128)(2,1)} %copy.67), kind=kOutput, calls=%fused_computation.52 | convolution fusion | flops 452984832 | bytes 3749888 | tf_op jit(solution)/shard_map/conv_general_dilated | solution.py:49
  347.8 1.0 fusion.26
  349.5 1.5 reshape.37
  351.0 5.3 %copy.60 = bf16[16,5,9,1,8,66]{0,4,5,2,1,3:T(8,128)(2,1)} copy(bf16[16,5,9,1,8,66]{5,4,0,2,1,3:T(8,128)(2,1)S(1)} %reshape.37) | data formatting | bytes 1520640 | tf_op jit(solution)/shard_map/conv_general_dilated | solution.py:37
  356.4 1.0 slice.48
  357.3 8.2 %fusion.19 = f32[2,4,8,33,64]{4,2,3,1,0:T(8,128)S(1)} fusion(bf16[3,3,3,16,64]{4,3,2,1,0:T(8,128)(2,1)} %bitcast.63, bf16[16,5,9,1,7,2]{0,4,5,2,1,3:T(8,128)(2,1)S(1)} %slice.48, bf16[16,5,9,1,8,66]{0,4,5,2,1,3:T(8,128)(2,1)} %copy.60, pred[8,33]{0,1:T(8,128)(4,1)S(1)} %copy-done.9), kind=kOutput, calls=%fused_computation.22 | convolution fusion | flops 119270400 | bytes 1376712 | tf_op jit(solution)/shard_map/conv_general_dilated | solution.py:37
  366.3 21.1 %copy.64 = bf16[1,16,5,9,513]{1,0,4,3,2:T(2,128)(2,1)} copy(bf16[1,16,5,9,513]{4,1,3,2,0:T(8,128)(2,1)S(1)} %get-tuple-element.16) | data formatting | bytes 1477440 | tf_op jit(solution)/shard_map/broadcast_in_dim | solution.py:84
  387.5 26.9 %fusion.37 = f32[3,3,3,16,64]{4,3,2,1,0:T(8,128)S(1)} fusion(bf16[1,16,5,9,513]{1,0,4,3,2:T(2,128)(2,1)} %copy.64, bf16[1,64,2,4,256]{1,0,4,3,2:T(2,128)(2,1)S(1)} %copy-done.4), kind=kOutput, calls=%fused_computation.51 | convolution fusion | flops 113246208 | bytes 1111456 | tf_op jit(solution)/shard_map/transpose | solution.py:90
  415.2 4.8 all-reduce.7
  420.8 64.0 %all-reduce.6.cloned.1.call-done = f32[41472]{0:T(1024)} async-done(((f32[41472]{0:T(1024)}), f32[41472]{0:T(1024)}) %all-reduce.6.cloned.1.call-update) | async-done | bytes 165904 | tf_op jit(solution)/shard_map/psum | solution.py:94
  (49 shorter events, 11.5 us)
Async XLA Ops:
  7.2 26.7 %copy-start = (bf16[27,32,64]{2,1,0:T(8,128)(2,1)S(1)}, bf16[27,32,64]{2,1,0:T(8,128)(2,1)}, u32[]{:S(2)}) copy-start(bf16[27,32,64]{2,1,0:T(8,128)(2,1)} %param.8) | copy-start | bytes 331780
  7.2 27.4 %copy-start.7 = (bf16[27,32,32]{2,1,0:T(8,128)(2,1)S(1)}, bf16[27,32,32]{2,1,0:T(8,128)(2,1)}, u32[]{:S(2)}) copy-start(bf16[27,32,32]{2,1,0:T(8,128)(2,1)} %param.9) | copy-start | bytes 165892
  7.2 30.8 %all-gather.2.cloned.1.call-start = ((), (), s32[]{:S(2)}) async-start(), calls=%async_computation | async-start | bytes 3145728 | tf_op jit(solution)/shard_map/all_gather | solution.py:70
  8.4 11.6 %collective-permute-start.1 = (bf16[16,2,8,512]{3,2,1,0:T(8,128)(2,1)S(1)}, bf16[16,2,8,512]{3,2,1,0:T(8,128)(2,1)S(1)}, u32[]{:S(2)}, u32[]{:S(2)}) collective-permute-start(bf16[16,2,8,512]{3,2,1,0:T(8,128)(2,1)S(1)} %get-tuple-element.21), channel_id=1, source_target_pairs={{2,0},{4,2},{6,4},{8,6},{10,8},{12,10},{14,12},{0,14},{3,1},{5,3},... | collective-permute-start | bytes 786440 | tf_op jit(solution)/shard_map/ppermute | solution.py:19
  14.4 10.5 %collective-permute-start = (bf16[16,2,8,512]{3,2,1,0:T(8,128)(2,1)S(1)}, bf16[16,2,8,512]{3,2,1,0:T(8,128)(2,1)S(1)}, u32[]{:S(2)}, u32[]{:S(2)}) collective-permute-start(bf16[16,2,8,512]{3,2,1,0:T(8,128)(2,1)S(1)} %get-tuple-element.20), channel_id=1, source_target_pairs={{0,2},{2,4},{4,6},{6,8},{8,10},{10,12},{12,14},{14,0},{1,3},{3,5},... | collective-permute-start | bytes 786440 | tf_op jit(solution)/shard_map/ppermute | solution.py:16
  27.1 457.7 %all-reduce.6.cloned.1.call-start = ((), (), s32[]{:S(2)}) async-start(), calls=%async_computation.1 | async-start | bytes 335872 | tf_op jit(solution)/shard_map/psum | solution.py:94
  58.4 18.8 %copy-start.8 = (pred[8,65]{0,1:T(8,128)(4,1)S(1)}, pred[8,65]{0,1:T(8,128)(4,1)}, u32[]{:S(2)}) copy-start(pred[8,65]{0,1:T(8,128)(4,1)} %constant.38) | copy-start | bytes 1564
  103.5 7.4 %copy-start.5 = (bf16[16,4,8,512]{3,2,1,0:T(8,128)(2,1)S(1)}, bf16[16,4,8,512]{3,2,1,0:T(8,128)(2,1)}, u32[]{:S(2)}) copy-start(bf16[16,4,8,512]{3,2,1,0:T(8,128)(2,1)} %param.6) | copy-start | bytes 1572868
  112.6 0.8 copy-start.2
  114.1 233.7 %collective-permute-start.2 = (bf16[16,1,8,512]{3,0,2,1:T(8,128)(2,1)}, bf16[16,1,8,512]{3,0,2,1:T(8,128)(2,1)}, u32[]{:S(2)}, u32[]{:S(2)}) collective-permute-start(bf16[16,1,8,512]{3,0,2,1:T(8,128)(2,1)} %slice.46), channel_id=1, source_target_pairs={{14,0},{0,2},{2,4},{4,6},{6,8},{8,10},{10,12},{12,14},{15,1},{1,3}... | collective-permute-start | bytes 393224 | tf_op jit(solution)/shard_map/ppermute | solution.py:27
  174.0 173.8 %copy-start.3 = (bf16[16,4,8,512]{3,0,2,1:T(8,128)(2,1)S(1)}, bf16[16,4,8,512]{3,0,2,1:T(8,128)(2,1)}, u32[]{:S(2)}) copy-start(bf16[16,4,8,512]{3,0,2,1:T(8,128)(2,1)} %copy-done.2) | copy-start | bytes 1572868
  349.4 7.9 %copy-start.9 = (pred[8,33]{0,1:T(8,128)(4,1)S(1)}, pred[8,33]{0,1:T(8,128)(4,1)}, u32[]{:S(2)}) copy-start(pred[8,33]{0,1:T(8,128)(4,1)} %constant.37) | copy-start | bytes 796
  366.3 21.1 %copy-start.4 = (bf16[1,64,2,4,256]{1,0,4,3,2:T(2,128)(2,1)S(1)}, bf16[1,64,2,4,256]{1,0,4,3,2:T(2,128)(2,1)}, u32[]{:S(2)}) copy-start(bf16[1,64,2,4,256]{1,0,4,3,2:T(2,128)(2,1)} %copy.65) | copy-start | bytes 786436
  387.5 27.1 %copy-start.6 = (f32[13824]{0:T(1024)S(1)}, f32[13824]{0:T(1024)}, u32[]{:S(2)}) copy-start(f32[13824]{0:T(1024)} %reshape_reshape.7) | copy-start | bytes 165892
  387.5 100.8 %copy-start.1 = (bf16[27,32,64]{2,1,0:T(8,128)(2,1)S(1)}, bf16[27,32,64]{2,1,0:T(8,128)(2,1)}, u32[]{:S(2)}) copy-start(bf16[27,32,64]{2,1,0:T(8,128)(2,1)} %param.8) | copy-start | bytes 331780
Sparse Core Ops, SparseCore 0:
  27.2 10.7 all-gather.1
  415.3 69.3 all-reduce.5
where the time goes:
time: 504 us; the launch traced here: 495 us
  matrix products  234 us (46%)
  local copies, waits for them, and re-layouts  142 us (28%)
  waiting for transfers between devices  77.7 us (15%)
  between operations  15.2 us (3%)
  other arithmetic  11.8 us (2%)
  starting transfers between devices  7.84 us (2%)
  blocking collectives  6.82 us (1%)
    conv_general_dilated x1, matrix products, filter_grad(): lax.conv_general_dilated(lhs, cotangent, window_strides=strides, padding=...  173 us
    psum x1, waiting for transfers between devices, local(): flat = lax.psum(flat, ('gz', 'sec'))  64 us
    broadcast_in_dim x2, local copies, waits for them, and re-layouts, local(): rimmed = wrap_y(rimmed, 2, 2)[None]  46.2 us
    conv_general_dilated x9, local copies, waits for them, and re-layouts, conv(): lax.conv_general_dilated(lhs, rhs, window_strides=strides, padding='VALID...  45.2 us
    conv_general_dilated x2, matrix products, conv(): lax.conv_general_dilated(lhs, rhs, window_strides=strides, padding='VALID...  34.5 us
    transpose x1, matrix products, local(): jnp.transpose(up_grad_k, (2, 3, 4, 1, 0))  26.9 us
    broadcast_in_dim x2, local copies, waits for them, and re-layouts, local(): extended = wrap_y(extended, 1, 0)[None]  21.2 us
    broadcast_in_dim x1, local copies, waits for them, and re-layouts, local(): refine_grad_k = filter_grad(rimmed, hidden[None], (2, 2, 2), (1, 1, 1))  14.3 us
  transfers between devices with their start and end apart: 5, of which 4 were waited for; matrix products, arithmetic and copies ran while one was open for 48% of the time, Pallas kernels for 0%

commit v1 on v0

--- a/solution.py
+++ b/solution.py
@@ -91,7 +91,7 @@
     coarse_summed = lax.psum_scatter(running[0], "ch", scatter_dimension=0, tiled=True)
     grad_coarse = coarse_summed.astype(jnp.bfloat16)
     flat = jnp.concatenate([up_terms.reshape(-1), refine_terms.reshape(-1)])
-    flat = lax.psum(flat, ("gz", "sec"))
+    flat = jnp.sum(lax.all_gather(flat, ("gz", "sec")), axis=0)
     up_summed = flat[: up_terms.size].reshape(up_terms.shape)
     refine_summed = flat[up_terms.size :].reshape(refine_terms.shape)
     fine_total = planes_z * lax.axis_size("gz") * lax.axis_size("sec") * planes_x * cells_y

time: 504 us -> 460 us (0.913)
  waiting for transfers between devices: 77.7 us -> 34.9 us
    psum x1 -> x0, waiting for transfers between devices: 64 us -> none  [local(): flat = lax.psum(flat, ('gz', 'sec'))]
    all_gather x0 -> x1, waiting for transfers between devices: none -> 18.6 us  [local(): flat = jnp.sum(lax.all_gather(flat, ('gz', 'sec')), axis=0)]
  transfers between devices with their start and end apart: 5 -> 5, of which waited for: 4 -> 4; matrix products, arithmetic and copies ran while one was open for 48% -> 56% of each run, Pallas kernels for 0% -> 0%
where the time goes in v1:
time: 460 us; the launch traced here: 451 us
  matrix products  234 us (51%)
  local copies, waits for them, and re-layouts  141 us (31%)
  waiting for transfers between devices  34.9 us (8%)
  between operations  15.2 us (3%)
  other arithmetic  11.7 us (3%)
  starting transfers between devices  7.84 us (2%)
  blocking collectives  6.82 us (1%)
    conv_general_dilated x1, matrix products, filter_grad(): lax.conv_general_dilated(lhs, cotangent, window_strides=strides, padding=...  173 us
    broadcast_in_dim x2, local copies, waits for them, and re-layouts, local(): rimmed = wrap_y(rimmed, 2, 2)[None]  46.2 us
    conv_general_dilated x9, local copies, waits for them, and re-layouts, conv(): lax.conv_general_dilated(lhs, rhs, window_strides=strides, padding='VALID...  45.2 us
    conv_general_dilated x2, matrix products, conv(): lax.conv_general_dilated(lhs, rhs, window_strides=strides, padding='VALID...  34.5 us
    transpose x1, matrix products, local(): jnp.transpose(up_grad_k, (2, 3, 4, 1, 0))  26.9 us
    broadcast_in_dim x2, local copies, waits for them, and re-layouts, local(): extended = wrap_y(extended, 1, 0)[None]  21.2 us
    all_gather x1, waiting for transfers between devices, local(): flat = jnp.sum(lax.all_gather(flat, ('gz', 'sec')), axis=0)  18.6 us
    broadcast_in_dim x1, local copies, waits for them, and re-layouts, local(): refine_grad_k = filter_grad(rimmed, hidden[None], (2, 2, 2), (1, 1, 1))  14.3 us
  transfers between devices with their start and end apart: 5, of which 4 were waited for; matrix products, arithmetic and copies ran while one was open for 56% of the time, Pallas kernels for 0%

profile of v1, /device:TPU:0, one launch (start us, length us, event | category | flops | bytes accessed | tf_op | source)
XLA Modules:
  0.0 451.5 jit_solution(1947083839620703508)
XLA Ops:
  7.2 1.2 fusion.36
  8.4 6.0 %collective-permute-start.1 = (bf16[16,2,8,512]{3,2,1,0:T(8,128)(2,1)S(1)}, bf16[16,2,8,512]{3,2,1,0:T(8,128)(2,1)S(1)}, u32[]{:S(2)}, u32[]{:S(2)}) collective-permute-start(bf16[16,2,8,512]{3,2,1,0:T(8,128)(2,1)S(1)} %get-tuple-element.21), channel_id=1, source_target_pairs={{2,0},{4,2},{6,4},{8,6},{10,8},{12,10},{14,12},{0,14},{3,1},{5,3},... | collective-permute-start | bytes 786440 | tf_op jit(solution)/shard_map/ppermute | solution.py:19
  14.4 5.6 %collective-permute-done.1 = bf16[16,2,8,512]{3,2,1,0:T(8,128)(2,1)S(1)} collective-permute-done((bf16[16,2,8,512]{3,2,1,0:T(8,128)(2,1)S(1)}, bf16[16,2,8,512]{3,2,1,0:T(8,128)(2,1)S(1)}, u32[]{:S(2)}, u32[]{:S(2)}) %collective-permute-start.1) | collective-permute-done | bytes 262176 | tf_op jit(solution)/shard_map/ppermute | solution.py:19
  20.0 4.9 %collective-permute-done = bf16[16,2,8,512]{3,2,1,0:T(8,128)(2,1)S(1)} collective-permute-done((bf16[16,2,8,512]{3,2,1,0:T(8,128)(2,1)S(1)}, bf16[16,2,8,512]{3,2,1,0:T(8,128)(2,1)S(1)}, u32[]{:S(2)}, u32[]{:S(2)}) %collective-permute-start) | collective-permute-done | bytes 262176 | tf_op jit(solution)/shard_map/ppermute | solution.py:16
  24.9 2.1 pad_maximum_fusion.1
  28.0 2.0 all_gather.13
  30.0 2.0 copy.65
  32.1 5.8 %all-gather.5.cloned.1.call-done = bf16[32,8,8,512]{3,2,1,0:T(8,128)(2,1)} async-done(((bf16[16,8,8,512]{3,2,1,0:T(8,128)(2,1)}), bf16[32,8,8,512]{3,2,1,0:T(8,128)(2,1)}) %all-gather.5.cloned.1.call-update) | async-done | bytes 2097168 | tf_op jit(solution)/shard_map/all_gather | solution.py:70
  37.9 2.5 copy.53
  41.1 4.0 fusion.23
  45.2 2.3 pad.10
  47.4 10.9 %reshape.30 = bf16[32,8,12,1,8,65]{5,4,1,2,0,3:T(8,128)(2,1)} reshape(bf16[32,8,12,1,520]{4,1,2,0,3:T(8,128)(2,1)} %pad.10) | data formatting | bytes 6389760 | tf_op jit(solution)/shard_map/conv_general_dilated | solution.py:37
  58.3 17.4 %copy.55 = bf16[32,8,12,1,8,65]{0,4,5,2,1,3:T(8,128)(2,1)} copy(bf16[32,8,12,1,8,65]{5,4,1,2,0,3:T(8,128)(2,1)} %reshape.30) | data formatting | bytes 6389760 | tf_op jit(solution)/shard_map/conv_general_dilated | solution.py:37
  75.7 1.4 slice.44
  77.1 26.3 %broadcast_select_fusion = f32[4,8,8,65,16]{4,2,3,1,0:T(8,128)} fusion(pred[8,65]{0,1:T(8,128)(4,1)S(1)} %copy-done.7, bf16[3,3,3,32,16]{4,3,2,1,0:T(8,128)(2,1)S(1)} %bitcast.62, bf16[32,8,12,1,7,4]{0,4,5,2,1,3:T(8,128)(2,1)S(1)} %slice.44, bf16[32,8,12,1,8,65]{0,4,5,2,1,3:T(8,128)(2,1)} %copy.55), kind=kOutput, calls=%fused_computation.14 | convolution fusion | flops 470503424 | bytes 4460040 | tf_op jit(solution)/shard_map/conv_general_dilated | solution.py:37
  103.4 5.6 %copy.57 = f32[4,8,8,65,16]{3,2,4,1,0:T(8,128)S(1)} copy(f32[4,8,8,65,16]{4,2,3,1,0:T(8,128)} %broadcast_select_fusion) | data formatting | bytes 2129920 | tf_op jit(solution)/shard_map/conv_general_dilated | solution.py:37
  109.1 1.8 reshape.34
  110.9 1.7 fusion.29
  114.1 1.7 collective-permute-start.2
  115.8 43.9 %copy.66 = bf16[1,32,8,12,516]{1,0,4,3,2:T(2,128)(2,1)} copy(bf16[1,32,8,12,516]{4,2,3,1,0:T(8,128)(2,1)} %get-tuple-element.12) | data formatting | bytes 6340608 | tf_op jit(solution)/shard_map/broadcast_in_dim | solution.py:72
  159.7 14.3 %copy.67 = bf16[1,16,4,8,512]{1,0,4,3,2:T(2,128)(2,1)} copy(bf16[1,16,4,8,512]{4,1,3,2,0:T(8,128)(2,1)S(1)} %get-tuple-element.18) | data formatting | bytes 1048576 | tf_op jit(solution)/shard_map/broadcast_in_dim | solution.py:77
  174.0 172.8 %fusion.38 = f32[16,32,3,3,3]{1,0,4,3,2:T(8,128)S(1)} fusion(bf16[1,32,8,12,516]{1,0,4,3,2:T(2,128)(2,1)} %copy.66, bf16[1,16,4,8,512]{1,0,4,3,2:T(2,128)(2,1)} %copy.67), kind=kOutput, calls=%fused_computation.52 | convolution fusion | flops 452984832 | bytes 3749888 | tf_op jit(solution)/shard_map/conv_general_dilated | solution.py:49
  347.3 1.0 fusion.26
  348.9 21.1 %copy.64 = bf16[1,16,5,9,513]{1,0,4,3,2:T(2,128)(2,1)} copy(bf16[1,16,5,9,513]{4,1,3,2,0:T(8,128)(2,1)S(1)} %get-tuple-element.16) | data formatting | bytes 1477440 | tf_op jit(solution)/shard_map/broadcast_in_dim | solution.py:84
  370.0 26.9 %fusion.37 = f32[3,3,3,16,64]{4,3,2,1,0:T(8,128)S(1)} fusion(bf16[1,16,5,9,513]{1,0,4,3,2:T(2,128)(2,1)} %copy.64, bf16[1,64,2,4,256]{1,0,4,3,2:T(2,128)(2,1)S(1)} %copy-done.3), kind=kOutput, calls=%fused_computation.51 | convolution fusion | flops 113246208 | bytes 1111456 | tf_op jit(solution)/shard_map/transpose | solution.py:90
  399.3 1.5 reshape.37
  400.8 5.3 %copy.60 = bf16[16,5,9,1,8,66]{0,4,5,2,1,3:T(8,128)(2,1)} copy(bf16[16,5,9,1,8,66]{5,4,0,2,1,3:T(8,128)(2,1)S(1)} %reshape.37) | data formatting | bytes 1520640 | tf_op jit(solution)/shard_map/conv_general_dilated | solution.py:37
  406.1 1.0 slice.48
  407.2 8.2 %fusion.19 = f32[2,4,8,33,64]{4,2,3,1,0:T(8,128)S(1)} fusion(bf16[3,3,3,16,64]{4,3,2,1,0:T(8,128)(2,1)S(1)} %bitcast.63, bf16[16,5,9,1,7,2]{0,4,5,2,1,3:T(8,128)(2,1)S(1)} %slice.48, bf16[16,5,9,1,8,66]{0,4,5,2,1,3:T(8,128)(2,1)} %copy.60, pred[8,33]{0,1:T(8,128)(4,1)S(1)} %copy-done.8), kind=kOutput, calls=%fused_computation.22 | convolution fusion | flops 119270400 | bytes 1376712 | tf_op jit(solution)/shard_map/conv_general_dilated | solution.py:37
  416.1 4.8 %all-reduce.4 = bf16[64,2,4,256]{3,2,1,0:T(4,128)(2,1)S(1)} all-reduce(f32[64,2,4,256]{3,2,1,0:T(4,128)S(1)} %copy.62), channel_id=3, replica_groups=mesh['groups'=2,'gz'=4,'sec'=2,'ch'=2] {'ch'}, use_global_device_ids=true, to_apply=%region_0.1.clone | all-reduce | flops 131072 | bytes 786432
  421.6 18.6 %all-gather.7.cloned.1.call-done = f32[8,1,41472]{2,1,0:T(1,128)} async-done(((f32[1,1,41472]{2,1,0:T(1,128)}), f32[8,1,41472]{2,1,0:T(1,128)}) %all-gather.7.cloned.1.call-update) | async-done | bytes 1327120 | tf_op jit(solution)/shard_map/all_gather | solution.py:94
  440.3 2.3 reduce_sum.9
  (49 shorter events, 9.3 us)
Async XLA Ops:
  7.2 392.0 %copy-start = (bf16[27,32,64]{2,1,0:T(8,128)(2,1)S(1)}, bf16[27,32,64]{2,1,0:T(8,128)(2,1)}, u32[]{:S(2)}) copy-start(bf16[27,32,64]{2,1,0:T(8,128)(2,1)} %param.8) | copy-start | bytes 331780
  7.2 24.8 %copy-start.5 = (bf16[27,32,32]{2,1,0:T(8,128)(2,1)S(1)}, bf16[27,32,32]{2,1,0:T(8,128)(2,1)}, u32[]{:S(2)}) copy-start(bf16[27,32,32]{2,1,0:T(8,128)(2,1)} %param.9) | copy-start | bytes 165892
  7.2 30.8 %all-gather.5.cloned.1.call-start = ((), (), s32[]{:S(2)}) async-start(), calls=%async_computation | async-start | bytes 3145728 | tf_op jit(solution)/shard_map/all_gather | solution.py:70
  8.4 11.6 %collective-permute-start.1 = (bf16[16,2,8,512]{3,2,1,0:T(8,128)(2,1)S(1)}, bf16[16,2,8,512]{3,2,1,0:T(8,128)(2,1)S(1)}, u32[]{:S(2)}, u32[]{:S(2)}) collective-permute-start(bf16[16,2,8,512]{3,2,1,0:T(8,128)(2,1)S(1)} %get-tuple-element.21), channel_id=1, source_target_pairs={{2,0},{4,2},{6,4},{8,6},{10,8},{12,10},{14,12},{0,14},{3,1},{5,3},... | collective-permute-start | bytes 786440 | tf_op jit(solution)/shard_map/ppermute | solution.py:19
  14.4 10.5 %collective-permute-start = (bf16[16,2,8,512]{3,2,1,0:T(8,128)(2,1)S(1)}, bf16[16,2,8,512]{3,2,1,0:T(8,128)(2,1)S(1)}, u32[]{:S(2)}, u32[]{:S(2)}) collective-permute-start(bf16[16,2,8,512]{3,2,1,0:T(8,128)(2,1)S(1)} %get-tuple-element.20), channel_id=1, source_target_pairs={{0,2},{2,4},{4,6},{6,8},{8,10},{10,12},{12,14},{14,0},{1,3},{3,5},... | collective-permute-start | bytes 786440 | tf_op jit(solution)/shard_map/ppermute | solution.py:16
  27.0 413.2 %all-gather.7.cloned.1.call-start = ((), (), s32[]{:S(2)}) async-start(), calls=%async_computation.1 | async-start | bytes 1492992 | tf_op jit(solution)/shard_map/all_gather | solution.py:94
  58.3 18.8 %copy-start.7 = (pred[8,65]{0,1:T(8,128)(4,1)S(1)}, pred[8,65]{0,1:T(8,128)(4,1)}, u32[]{:S(2)}) copy-start(pred[8,65]{0,1:T(8,128)(4,1)} %constant.39) | copy-start | bytes 1564
  103.4 7.4 %copy-start.4 = (bf16[16,4,8,512]{3,2,1,0:T(8,128)(2,1)S(1)}, bf16[16,4,8,512]{3,2,1,0:T(8,128)(2,1)}, u32[]{:S(2)}) copy-start(bf16[16,4,8,512]{3,2,1,0:T(8,128)(2,1)} %param.6) | copy-start | bytes 1572868
  112.6 0.8 copy-start.1
  114.1 233.2 %collective-permute-start.2 = (bf16[16,1,8,512]{3,0,2,1:T(8,128)(2,1)}, bf16[16,1,8,512]{3,0,2,1:T(8,128)(2,1)}, u32[]{:S(2)}, u32[]{:S(2)}) collective-permute-start(bf16[16,1,8,512]{3,0,2,1:T(8,128)(2,1)} %slice.46), channel_id=1, source_target_pairs={{14,0},{0,2},{2,4},{4,6},{6,8},{8,10},{10,12},{12,14},{15,1},{1,3}... | collective-permute-start | bytes 393224 | tf_op jit(solution)/shard_map/ppermute | solution.py:27
  174.0 173.3 %copy-start.2 = (bf16[16,4,8,512]{3,0,2,1:T(8,128)(2,1)S(1)}, bf16[16,4,8,512]{3,0,2,1:T(8,128)(2,1)}, u32[]{:S(2)}) copy-start(bf16[16,4,8,512]{3,0,2,1:T(8,128)(2,1)} %copy-done.1) | copy-start | bytes 1572868
  348.9 21.1 %copy-start.3 = (bf16[1,64,2,4,256]{1,0,4,3,2:T(2,128)(2,1)S(1)}, bf16[1,64,2,4,256]{1,0,4,3,2:T(2,128)(2,1)}, u32[]{:S(2)}) copy-start(bf16[1,64,2,4,256]{1,0,4,3,2:T(2,128)(2,1)} %copy.65) | copy-start | bytes 786436
  370.0 27.9 %copy-start.6 = (u32[32]{0:T(128)S(1)}, u32[32]{0:T(128)}, u32[]{:S(2)}) copy-start(u32[32]{0:T(128)} %constant.42) | copy-start | bytes 388
  397.9 9.3 %copy-start.8 = (pred[8,33]{0,1:T(8,128)(4,1)S(1)}, pred[8,33]{0,1:T(8,128)(4,1)}, u32[]{:S(2)}) copy-start(pred[8,33]{0,1:T(8,128)(4,1)} %constant.38) | copy-start | bytes 796
Sparse Core Ops, SparseCore 0:
  27.2 10.7 all-gather.4
  398.0 42.1 all-gather.6
